TPU v7x, 256 devices: a whole 4x4x8 slice. The times are simulated.
256 devices in a mesh: tile: 128 (over z, x, y), chan: 2 (over core).
Axes of the slice: x: 4, y: 4, z: 8, core: 2. Of those that a mesh axis runs over, the one named last changes fastest.
Arguments:
- jacobian: bfloat16 [1024, 616, 411], P('tile', 'chan'), may hold values from -0.3125 to 0.3125
- r_inverse: bfloat16 [616, 616], P('chan'), as said below
- innovation: bfloat16 [1024, 616], P('tile', 'chan'), may hold values from -6 to 6
- increments: bfloat16 [2048, 128, 411], P('tile'), may hold values from -6 to 6
- owner_offset: int32 [1024, 1], P('tile'), may hold values from 0 to 3; in each aligned block of 8 rows (0 to 7, 8 to 15, ...) at most 3 rows name the same one
- column_slot: int32 [1024], P('tile'), may hold values from 0 to 15
- foot_counts: int32 [128], P('tile'), may hold values from 1 to 8, as said below
Outputs:
- gradient: bfloat16 [2048, 128, 411], P('tile')
Inputs may be any that keep to these rules, and one draw needn't show every extreme that they name: r_inverse is symmetric. `owner_offset`: the 8 footprints of one tile name each value at most 3 times, and some tile names some value exactly 3 times. `foot_counts`: each count is 8 divided by 1, 2, 4 or 8; some tile has 8.
All inputs are finite; a program needn't handle non-finite values.
Results may differ from a plain program's by a relative error of at most 0.0052.
Values may be sent and summed in bfloat16 or wider, within the bound.
No kernel may reach another device: no remote copies, remote signals or barrier semaphores. Data moves between devices by JAX's collectives and lax.ppermute only.
A program may use at most 64 MiB of HBM per device.

v0:
```python
import jax
import jax.numpy as jnp
from jax import lax
from jax.sharding import PartitionSpec as P

SPAN = 4
CAP = 3
group_rows = 8


def passed_along(value, axis, by):
    count = lax.axis_size(axis)
    return lax.ppermute(value, axis, [(i, (i + by) % count) for i in range(count)])


def on_device(jacobian, r_inverse, innovation, increments, owner_offset, column_slot, foot_counts):
    foot = jacobian.shape[0]
    state = jacobian.shape[2]
    columns = increments.shape[0]
    members = increments.shape[1]
    capacity = CAP
    slots_total = SPAN * capacity
    offset = owner_offset[:, 0]
    order = jnp.arange(foot, dtype=jnp.int32)
    earlier = (offset[:, None] == offset[None, :]) & (order[None, :] < order[:, None])
    rank = jnp.sum(earlier.astype(jnp.int32), axis=1)
    place = offset * capacity + rank
    select = place[None, :] == jnp.arange(slots_total, dtype=jnp.int32)[:, None]
    request = jnp.sum(jnp.where(select, column_slot[None, :], 0), axis=1)
    jac_all, innov_all, r_all = (jacobian, innovation, r_inverse)
    fetched_parts = []
    for neighbor_rank in range(SPAN):
        wanted = request[neighbor_rank * capacity : (neighbor_rank + 1) * capacity]
        if neighbor_rank == 1:
            fetched_parts.append(jnp.take(increments, wanted, axis=0))
        else:
            asked = passed_along(wanted, "tile", neighbor_rank - 1)
            picked = jnp.take(increments, asked, axis=0)
            fetched_parts.append(passed_along(picked, "tile", 1 - neighbor_rank))
    fetched = jnp.concatenate(fetched_parts, axis=0)
    column_state = jnp.take(fetched, place, axis=0)
    count = foot_counts[0]
    block_total = (count + group_rows - 1) // group_rows
    adjoint_buf = jnp.zeros((foot, members, state), jnp.bfloat16)

    def one_block(block_index, buf):
        start = block_index * group_rows
        evolved = jnp.einsum(
            "fks,fms->fmk", jac_all, column_state, preferred_element_type=jnp.float32
        )
        departure = (evolved - innov_all.astype(jnp.float32)[:, None, :]).astype(jnp.bfloat16)
        all_channels = lax.all_gather(departure, "chan", axis=2, tiled=True)
        weighted = jnp.einsum(
            "fmk,ik->fmi", all_channels, r_all, preferred_element_type=jnp.float32
        )
        weighted = weighted.astype(jnp.bfloat16)
        partial_adj = jnp.einsum(
            "fks,fmk->fms", jac_all, weighted, preferred_element_type=jnp.float32
        )
        summed = lax.psum(partial_adj, "chan")
        live = start + jnp.arange(group_rows, dtype=jnp.int32) < count
        summed = jnp.where(live[:, None, None], summed, jnp.zeros_like(summed)).astype(jnp.bfloat16)
        return summed

    adjoint_buf = lax.fori_loop(0, block_total, one_block, adjoint_buf)
    flat = adjoint_buf.reshape(foot, members * state)
    packed = jnp.dot(select.astype(jnp.bfloat16), flat, preferred_element_type=jnp.float32).astype(
        jnp.bfloat16
    )
    received_parts = []
    slot_parts = []
    for neighbor_rank in range(SPAN):
        piece = packed[neighbor_rank * capacity : (neighbor_rank + 1) * capacity]
        wanted = request[neighbor_rank * capacity : (neighbor_rank + 1) * capacity]
        if neighbor_rank == 1:
            received_parts.append(piece)
            slot_parts.append(wanted)
        else:
            moved, moved_slots = passed_along((piece, wanted), "tile", neighbor_rank - 1)
            received_parts.append(moved)
            slot_parts.append(moved_slots)
    received = jnp.concatenate(received_parts, axis=0)
    got_slots = jnp.concatenate(slot_parts, axis=0)
    assign = (got_slots[None, :] == jnp.arange(columns, dtype=jnp.int32)[:, None]).astype(
        jnp.bfloat16
    )
    gradient = jnp.dot(assign, received, preferred_element_type=jnp.float32).astype(jnp.bfloat16)
    gradient = gradient.reshape(columns, members, state)
    return gradient


def solution(mesh):
    in_specs = (
        P("tile", "chan", None),
        P("chan", None),
        P("tile", "chan"),
        P("tile", None, None),
        P("tile", None),
        P("tile"),
        P("tile"),
    )
    out_specs = P("tile", None, None)
    return jax.shard_map(
        on_device, mesh=mesh, in_specs=in_specs, out_specs=out_specs, check_vma=False
    )
```

profile of v0, /device:TPU:8, one launch (start us, length us, event | category | flops | bytes accessed | tf_op | source)
XLA Modules:
  0.0 157.8 jit_solution(7195260682323156579)
XLA Ops:
  6.5 1.0 convert_reduce_fusion
  7.5 0.7 multiply_add_fusion
  8.2 0.7 select_reduce_fusion
  8.9 0.1 fusion.22
  9.0 2.2 %collective-permute-start = (s32[3]{0:T(128)S(1)}, s32[3]{0:T(128)S(1)}, u32[]{:S(2)}, u32[]{:S(2)}) collective-permute-start(s32[3]{0:T(128)S(1)} %get-tuple-element.221), channel_id=1, source_target_pairs={{0,254},{2,0},{4,2},{6,4},{8,6},{10,8},{12,10},{14,12},{16,14},{18... | collective-permute-start | bytes 44 | tf_op jit(solution)/shard_map/ppermute | solution.py:13
  11.2 4.3 %collective-permute-start.2 = (s32[3]{0:T(128)S(1)}, s32[3]{0:T(128)S(1)}, u32[]{:S(2)}, u32[]{:S(2)}) collective-permute-start(s32[3]{0:T(128)S(1)} %get-tuple-element.219), channel_id=1, source_target_pairs={{0,4},{2,6},{4,8},{6,10},{8,12},{10,14},{12,16},{14,18},{16,20},{1... | collective-permute-start | bytes 44 | tf_op jit(solution)/shard_map/ppermute | solution.py:13
  15.4 0.1 compare_and_fusion.2
  15.5 0.7 and_bitcast_fusion
  16.2 4.5 %copy.26 = bf16[8,308,411]{1,2,0:T(8,128)(2,1)} copy(bf16[8,308,411]{2,0,1:T(8,128)(2,1)} %param.11) | data formatting | bytes 4050816 | tf_op args[0]
  20.8 2.5 %gather_fusion.2 = bf16[3,128,411]{1,0,2:T(4,128)(2,1)S(1)} fusion(bf16[16,128,411]{1,0,2:T(8,128)(2,1)S(1)} %copy-done, s32[1024]{0:T(1024)S(1)} %pad_clamp_fusion.3), kind=kCustom, calls=%fused_computation.1.clone | custom fusion | bytes 631308 | tf_op jit(solution)/shard_map/jit(_take)/gather | solution.py:35
  23.3 2.5 %gather_fusion.1 = bf16[3,128,411]{1,0,2:T(4,128)(2,1)S(1)} fusion(bf16[16,128,411]{1,0,2:T(8,128)(2,1)S(1)} %copy-done, s32[1024]{0:T(1024)S(1)} %pad_clamp_fusion.4), kind=kCustom, calls=%fused_computation.clone | custom fusion | bytes 631308 | tf_op jit(solution)/shard_map/jit(_take)/gather | solution.py:38
  25.7 1.0 broadcast_select_fusion.3
  26.8 2.5 %gather_fusion.3 = bf16[3,128,411]{1,0,2:T(4,128)(2,1)S(1)} fusion(bf16[16,128,411]{1,0,2:T(8,128)(2,1)S(1)} %copy-done, s32[1024]{0:T(1024)S(1)} %pad_clamp_fusion.2), kind=kCustom, calls=%fused_computation.2.clone | custom fusion | bytes 631308 | tf_op jit(solution)/shard_map/jit(_take)/gather | solution.py:38
  29.3 1.0 broadcast_select_fusion.1
  30.3 4.5 %collective-permute-start.4 = (bf16[3,128,411]{1,0,2:T(4,128)(2,1)}, bf16[3,128,411]{1,0,2:T(4,128)(2,1)S(1)}, u32[]{:S(2)}, u32[]{:S(2)}) collective-permute-start(bf16[3,128,411]{1,0,2:T(4,128)(2,1)} %broadcast_select_fusion.1), channel_id=1, source_target_pairs={{0,254},{2,0},{4,2},{6,4},{8,6},{10,8},{12,10},{14,12},{16,14},{18... | collective-permute-start | bytes 946952 | tf_op jit(solution)/shard_map/ppermute | solution.py:13
  34.8 2.5 %gather_fusion.4 = bf16[3,128,411]{1,0,2:T(4,128)(2,1)S(1)} fusion(bf16[16,128,411]{1,0,2:T(8,128)(2,1)S(1)} %copy-done, s32[1024]{0:T(1024)S(1)} %pad_clamp_fusion.1), kind=kCustom, calls=%fused_computation.3.clone | custom fusion | bytes 631308 | tf_op jit(solution)/shard_map/jit(_take)/gather | solution.py:38
  37.3 0.2 broadcast_select_fusion
  37.5 8.4 %collective-permute-start.5 = (bf16[3,128,411]{1,0,2:T(4,128)(2,1)S(1)}, bf16[3,128,411]{1,0,2:T(4,128)(2,1)S(1)}, u32[]{:S(2)}, u32[]{:S(2)}) collective-permute-start(bf16[3,128,411]{1,0,2:T(4,128)(2,1)S(1)} %broadcast_select_fusion), channel_id=1, source_target_pairs={{0,252},{2,254},{4,0},{6,2},{8,4},{10,6},{12,8},{14,10},{16,12},{1... | collective-permute-start | bytes 946952 | tf_op jit(solution)/shard_map/ppermute | solution.py:13
  45.9 0.2 broadcast_select_fusion.2
  46.1 6.7 %collective-permute-done.4 = bf16[3,128,411]{1,0,2:T(4,128)(2,1)S(1)} collective-permute-done((bf16[3,128,411]{1,0,2:T(4,128)(2,1)}, bf16[3,128,411]{1,0,2:T(4,128)(2,1)S(1)}, u32[]{:S(2)}, u32[]{:S(2)}) %collective-permute-start.4) | collective-permute-done | bytes 315680 | tf_op jit(solution)/shard_map/ppermute | solution.py:13
  52.8 4.7 %collective-permute-done.5 = bf16[3,128,411]{1,0,2:T(4,128)(2,1)S(1)} collective-permute-done((bf16[3,128,411]{1,0,2:T(4,128)(2,1)S(1)}, bf16[3,128,411]{1,0,2:T(4,128)(2,1)S(1)}, u32[]{:S(2)}, u32[]{:S(2)}) %collective-permute-start.5) | collective-permute-done | bytes 315680 | tf_op jit(solution)/shard_map/ppermute | solution.py:13
  57.5 1.4 pad_maximum_fusion
  58.8 0.3 copy.22
  59.2 1.6 gather_fusion
  60.7 3.3 %fusion.7 = bf16[8,128,308]{1,2,0:T(8,128)(2,1)S(1)} fusion(bf16[8,308,411]{1,2,0:T(8,128)(2,1)} %copy.26, bf16[8,128,411]{1,2,0:T(8,128)(2,1)} %gather_fusion, pred[8]{0:T(512)(128)(4,1)S(1)} %get-tuple-element.210, f32[8,308]{1,0:T(8,128)S(1)} %convert_element_type.46), kind=kOutput, calls=%fused_computation.18 | convolution fusion | flops 260303872 | bytes 3507784 | tf_op jit(solution)/shard_map/while/body/fks,fms->fmk/dot_general | solution.py:48
  64.0 0.9 copy.24
  64.9 0.0 all-gather.2.cloned.1.call-update
  65.6 15.6 %all-gather.2.cloned.1.call-done = bf16[8,128,616]{1,0,2:T(8,128)(2,1)} async-done(((bf16[8,128,308]{1,0,2:T(8,128)(2,1)}), bf16[8,128,616]{1,0,2:T(8,128)(2,1)}) %all-gather.2.cloned.1.call-update) | async-done | bytes 1261584 | tf_op jit(solution)/shard_map/while/body/all_gather | solution.py:52
  81.2 3.6 %fusion.8 = f32[8,128,411]{1,2,0:T(8,128)S(1)} fusion(bf16[8,308,411]{1,2,0:T(8,128)(2,1)} %copy.26, bf16[8,128,616]{1,0,2:T(8,128)(2,1)} %all-gather.2.cloned.1.call-done, bf16[308,616]{1,0:T(8,128)(2,1)} %param.12), kind=kOutput, calls=%fused_computation.20 | convolution fusion | flops 648130560 | bytes 5349888 | tf_op jit(solution)/shard_map/while/body/fks,fmk->fms/dot_general | solution.py:57
  84.8 8.4 %all-reduce.1 = bf16[8,128,411]{1,2,0:T(8,128)(2,1)} all-reduce(f32[8,128,411]{1,2,0:T(8,128)S(1)} %fusion.8), channel_id=1, replica_groups=mesh['tile'=128,'chan'=2] {'chan'}, use_global_device_ids=true, to_apply=%region_2.4 | all-reduce | flops 420864 | bytes 2525184 | tf_op jit(solution)/shard_map/while/body/psum | solution.py:60
  93.3 1.4 copy.27
  94.7 1.1 broadcast_in_dim.60
  95.8 2.0 %while.16 = (s32[]{:T(128)}, bf16[8,128,411]{2,1,0:T(8,128)(2,1)}, s32[]{:T(128)}, s32[]{:T(128)}, bf16[8,128,411]{2,1,0:T(8,128)(2,1)S(1)}, /*index=5*/s32[]{:T(128)}, s32[]{:T(128)}) while((s32[]{:T(128)}, bf16[8,128,411]{2,1,0:T(8,128)(2,1)}, s32[]{:T(128)}, s32[]{:T(128)}, bf16[8,128,411]{2,1,0:T(8,128)(2,1)S(1)}, /*index=5*/s32[]{:T(128)}, ...), condition=%wide.region_4.6_spmd, body=%wide.region_3.5_spmd.sunk | while | flops 420883 | bytes 1683569 | solution.py:65
  95.8 0.7 add_compare_fusion.2
  96.4 1.3 select_convert_fusion.2
  97.8 2.6 %reshape.37 = bf16[8,52608]{1,0:T(8,128)(2,1)S(1)} reshape(bf16[8,128,411]{2,1,0:T(8,128)(2,1)} %get-tuple-element.179) | data formatting | bytes 1683456 | tf_op jit(solution)/shard_map/reshape | solution.py:66
  100.4 0.7 convolution_convert_fusion.1
  101.1 0.7 fusion.21
  101.8 1.1 collective-permute-start.6
  102.9 1.2 collective-permute-start.7
  104.1 4.2 %collective-permute-start.8 = (bf16[3,52608]{1,0:T(4,128)(2,1)S(1)}, bf16[3,52608]{1,0:T(4,128)(2,1)S(1)}, u32[]{:S(2)}, u32[]{:S(2)}) collective-permute-start(bf16[3,52608]{1,0:T(4,128)(2,1)S(1)} %get-tuple-element.215), channel_id=1, source_target_pairs={{0,4},{2,6},{4,8},{6,10},{8,12},{10,14},{12,16},{14,18},{16,20},{1... | collective-permute-start | bytes 946952 | tf_op jit(solution)/shard_map/ppermute | solution.py:13
  108.3 0.1 pad_add_fusion
  108.4 5.5 %collective-permute-done.6 = bf16[3,52608]{1,0:T(4,128)(2,1)S(1)} collective-permute-done((bf16[3,52608]{1,0:T(4,128)(2,1)S(1)}, bf16[3,52608]{1,0:T(4,128)(2,1)S(1)}, u32[]{:S(2)}, u32[]{:S(2)}) %collective-permute-start.6) | collective-permute-done | bytes 315680 | tf_op jit(solution)/shard_map/ppermute | solution.py:13
  113.9 6.9 %collective-permute-done.7 = bf16[3,52608]{1,0:T(4,128)(2,1)S(1)} collective-permute-done((bf16[3,52608]{1,0:T(4,128)(2,1)S(1)}, bf16[3,52608]{1,0:T(4,128)(2,1)S(1)}, u32[]{:S(2)}, u32[]{:S(2)}) %collective-permute-start.7) | collective-permute-done | bytes 315680 | tf_op jit(solution)/shard_map/ppermute | solution.py:13
  120.8 19.4 %collective-permute-done.8 = bf16[3,52608]{1,0:T(4,128)(2,1)S(1)} collective-permute-done((bf16[3,52608]{1,0:T(4,128)(2,1)S(1)}, bf16[3,52608]{1,0:T(4,128)(2,1)S(1)}, u32[]{:S(2)}, u32[]{:S(2)}) %collective-permute-start.8) | collective-permute-done | bytes 315680 | tf_op jit(solution)/shard_map/ppermute | solution.py:13
  140.2 1.4 convolution_convert_fusion
  141.6 5.0 %reshape.38 = bf16[16,128,411]{2,1,0:T(8,128)(2,1)} reshape(bf16[16,52608]{1,0:T(8,128)(2,1)S(1)} %convolution_convert_fusion) | data formatting | bytes 3366912 | tf_op jit(solution)/shard_map/reshape | solution.py:88
  146.6 4.3 %copy.28 = bf16[16,128,411]{1,0,2:T(8,128)(2,1)} copy(bf16[16,128,411]{2,1,0:T(8,128)(2,1)} %reshape.38) | data formatting | bytes 3366912 | tf_op jit(solution)/shard_map/reshape | solution.py:88
  (23 shorter events, 0.1 us)
Async XLA Ops:
  6.5 14.2 %copy-start = (bf16[16,128,411]{1,0,2:T(8,128)(2,1)S(1)}, bf16[16,128,411]{1,0,2:T(8,128)(2,1)}, u32[]{:S(2)}) copy-start(bf16[16,128,411]{1,0,2:T(8,128)(2,1)} %param.14) | copy-start | bytes 5050372
  6.5 74.7 %all-gather.2.cloned.1.call-start = ((), (), s32[]{:S(2)}) async-start(), calls=%async_computation | async-start | bytes 1892352 | tf_op jit(solution)/shard_map/while/body/all_gather | solution.py:52
  9.0 14.2 %collective-permute-start = (s32[3]{0:T(128)S(1)}, s32[3]{0:T(128)S(1)}, u32[]{:S(2)}, u32[]{:S(2)}) collective-permute-start(s32[3]{0:T(128)S(1)} %get-tuple-element.221), channel_id=1, source_target_pairs={{0,254},{2,0},{4,2},{6,4},{8,6},{10,8},{12,10},{14,12},{16,14},{18... | collective-permute-start | bytes 44 | tf_op jit(solution)/shard_map/ppermute | solution.py:13
  11.2 15.6 %collective-permute-start.1 = (s32[3]{0:T(128)S(1)}, s32[3]{0:T(128)S(1)}, u32[]{:S(2)}, u32[]{:S(2)}) collective-permute-start(s32[3]{0:T(128)S(1)} %get-tuple-element.220), channel_id=1, source_target_pairs={{0,2},{2,4},{4,6},{6,8},{8,10},{10,12},{12,14},{14,16},{16,18},{18... | collective-permute-start | bytes 44 | tf_op jit(solution)/shard_map/ppermute | solution.py:13
  11.2 23.6 %collective-permute-start.2 = (s32[3]{0:T(128)S(1)}, s32[3]{0:T(128)S(1)}, u32[]{:S(2)}, u32[]{:S(2)}) collective-permute-start(s32[3]{0:T(128)S(1)} %get-tuple-element.219), channel_id=1, source_target_pairs={{0,4},{2,6},{4,8},{6,10},{8,12},{10,14},{12,16},{14,18},{16,20},{1... | collective-permute-start | bytes 44 | tf_op jit(solution)/shard_map/ppermute | solution.py:13
  16.2 4.6 %copy-start.1 = (bf16[8,308]{1,0:T(8,128)(2,1)S(1)}, bf16[8,308]{1,0:T(8,128)(2,1)}, u32[]{:S(2)}) copy-start(bf16[8,308]{1,0:T(8,128)(2,1)} %param.13) | copy-start | bytes 14788
  26.8 19.4 %collective-permute-start.3 = (bf16[3,128,411]{1,0,2:T(4,128)(2,1)}, bf16[3,128,411]{1,0,2:T(4,128)(2,1)S(1)}, u32[]{:S(2)}, u32[]{:S(2)}) collective-permute-start(bf16[3,128,411]{1,0,2:T(4,128)(2,1)} %broadcast_select_fusion.3), channel_id=1, source_target_pairs={{0,2},{2,4},{4,6},{6,8},{8,10},{10,12},{12,14},{14,16},{16,18},{18... | collective-permute-start | bytes 946952 | tf_op jit(solution)/shard_map/ppermute | solution.py:13
  30.3 22.5 %collective-permute-start.4 = (bf16[3,128,411]{1,0,2:T(4,128)(2,1)}, bf16[3,128,411]{1,0,2:T(4,128)(2,1)S(1)}, u32[]{:S(2)}, u32[]{:S(2)}) collective-permute-start(bf16[3,128,411]{1,0,2:T(4,128)(2,1)} %broadcast_select_fusion.1), channel_id=1, source_target_pairs={{0,254},{2,0},{4,2},{6,4},{8,6},{10,8},{12,10},{14,12},{16,14},{18... | collective-permute-start | bytes 946952 | tf_op jit(solution)/shard_map/ppermute | solution.py:13
  37.5 19.9 %collective-permute-start.5 = (bf16[3,128,411]{1,0,2:T(4,128)(2,1)S(1)}, bf16[3,128,411]{1,0,2:T(4,128)(2,1)S(1)}, u32[]{:S(2)}, u32[]{:S(2)}) collective-permute-start(bf16[3,128,411]{1,0,2:T(4,128)(2,1)S(1)} %broadcast_select_fusion), channel_id=1, source_target_pairs={{0,252},{2,254},{4,0},{6,2},{8,4},{10,6},{12,8},{14,10},{16,12},{1... | collective-permute-start | bytes 946952 | tf_op jit(solution)/shard_map/ppermute | solution.py:13
  101.8 12.1 %collective-permute-start.6 = (bf16[3,52608]{1,0:T(4,128)(2,1)S(1)}, bf16[3,52608]{1,0:T(4,128)(2,1)S(1)}, u32[]{:S(2)}, u32[]{:S(2)}) collective-permute-start(bf16[3,52608]{1,0:T(4,128)(2,1)S(1)} %get-tuple-element.214), channel_id=1, source_target_pairs={{0,254},{2,0},{4,2},{6,4},{8,6},{10,8},{12,10},{14,12},{16,14},{18... | collective-permute-start | bytes 946952 | tf_op jit(solution)/shard_map/ppermute | solution.py:13
  102.9 17.9 %collective-permute-start.7 = (bf16[3,52608]{1,0:T(4,128)(2,1)S(1)}, bf16[3,52608]{1,0:T(4,128)(2,1)S(1)}, u32[]{:S(2)}, u32[]{:S(2)}) collective-permute-start(bf16[3,52608]{1,0:T(4,128)(2,1)S(1)} %get-tuple-element.216), channel_id=1, source_target_pairs={{0,2},{2,4},{4,6},{6,8},{8,10},{10,12},{12,14},{14,16},{16,18},{18... | collective-permute-start | bytes 946952 | tf_op jit(solution)/shard_map/ppermute | solution.py:13
  104.1 36.1 %collective-permute-start.8 = (bf16[3,52608]{1,0:T(4,128)(2,1)S(1)}, bf16[3,52608]{1,0:T(4,128)(2,1)S(1)}, u32[]{:S(2)}, u32[]{:S(2)}) collective-permute-start(bf16[3,52608]{1,0:T(4,128)(2,1)S(1)} %get-tuple-element.215), channel_id=1, source_target_pairs={{0,4},{2,6},{4,8},{6,10},{8,12},{10,14},{12,16},{14,18},{16,20},{1... | collective-permute-start | bytes 946952 | tf_op jit(solution)/shard_map/ppermute | solution.py:13
Sparse Core Ops, SparseCore 0:
  65.1 16.1 all-gather.1
where the time goes:
time: 158 us
  waiting for transfers between devices  58.7 us (37%)
  local copies, waits for them, and re-layouts  32.4 us (21%)
  starting transfers between devices  25.9 us (16%)
  between operations  14.2 us (9%)
  other arithmetic  9.06 us (6%)
  matrix products  9.01 us (6%)
  blocking collectives  8.43 us (5%)
    ppermute x9, waiting for transfers between devices, passed_along(): lax.ppermute(value, axis, [(i, (i + by) % count) for i in range(count)])  43.1 us
    ppermute x9, starting transfers between devices, passed_along(): lax.ppermute(value, axis, [(i, (i + by) % count) for i in range(count)])  25.9 us
    all_gather x1, waiting for transfers between devices, one_block(): all_channels = lax.all_gather(departure, 'chan', axis=2, tiled=True)  15.6 us
    reshape x2, local copies, waits for them, and re-layouts, on_device(): gradient = gradient.reshape(columns, members, state)  9.34 us
    psum x1, blocking collectives, one_block(): summed = lax.psum(partial_adj, 'chan')  8.43 us
    gather x3, local copies, waits for them, and re-layouts, on_device(): picked = jnp.take(increments, asked, axis=0)  7.38 us
    unnamed x5, local copies, waits for them, and re-layouts  4.56 us
    dot_general x1, matrix products, one_block(): jnp.einsum('fks,fmk->fms', jac_all, weighted, preferred_element_type=jnp....  3.6 us
  transfers between devices with their start and end apart: 10, of which 6 were waited for; matrix products, arithmetic and copies ran while one was open for 11% of the time, Pallas kernels for 0%

commit v1 on v0

--- a/solution.py
+++ b/solution.py
@@ -57,7 +57,7 @@
         partial_adj = jnp.einsum(
             "fks,fmk->fms", jac_all, weighted, preferred_element_type=jnp.float32
         )
-        summed = lax.psum(partial_adj, "chan")
+        summed = lax.all_gather(partial_adj, "chan").sum(axis=0)
         live = start + jnp.arange(group_rows, dtype=jnp.int32) < count
         summed = jnp.where(live[:, None, None], summed, jnp.zeros_like(summed)).astype(jnp.bfloat16)
         return summed

time: 158 us -> 174 us (1.10)
  waiting for transfers between devices: 58.7 us -> 77.3 us
  blocking collectives: 8.43 us -> 0 us
  other arithmetic: 9.06 us -> 12.4 us
  local copies, waits for them, and re-layouts: 32.4 us -> 34.7 us
    all_gather x0 -> x1, waiting for transfers between devices: none -> 17.9 us  [one_block(): summed = lax.all_gather(partial_adj, 'chan').sum(axis=0)]
    psum x1 -> x0, blocking collectives: 8.43 us -> none  [one_block(): summed = lax.psum(partial_adj, 'chan')]
    reduce_sum x0 -> x1, other arithmetic: none -> 3.34 us  [one_block(): summed = lax.all_gather(partial_adj, 'chan').sum(axis=0)]
    dot_general x0 -> x1, local copies, waits for them, and re-layouts: none -> 2.16 us  [one_block(): jnp.einsum('fks,fmk->fms', jac_all, weighted, preferred_element_type=jnp....]
  transfers between devices with their start and end apart: 10 -> 11, of which waited for: 6 -> 7; matrix products, arithmetic and copies ran while one was open for 11% -> 10% of each run, Pallas kernels for 0% -> 0%
where the time goes in v1:
time: 174 us; the launch traced here: 173 us
  waiting for transfers between devices  77.3 us (44%)
  local copies, waits for them, and re-layouts  34.7 us (20%)
  starting transfers between devices  25.7 us (15%)
  between operations  14.3 us (8%)
  other arithmetic  12.4 us (7%)
  matrix products  9.01 us (5%)
    ppermute x9, waiting for transfers between devices, passed_along(): lax.ppermute(value, axis, [(i, (i + by) % count) for i in range(count)])  43.1 us
    ppermute x9, starting transfers between devices, passed_along(): lax.ppermute(value, axis, [(i, (i + by) % count) for i in range(count)])  25.7 us
    all_gather x1, waiting for transfers between devices, one_block(): summed = lax.all_gather(partial_adj, 'chan').sum(axis=0)  17.9 us
    all_gather x1, waiting for transfers between devices, one_block(): all_channels = lax.all_gather(departure, 'chan', axis=2, tiled=True)  16.2 us
    reshape x2, local copies, waits for them, and re-layouts, on_device(): gradient = gradient.reshape(columns, members, state)  9.32 us
    gather x3, local copies, waits for them, and re-layouts, on_device(): picked = jnp.take(increments, asked, axis=0)  7.38 us
    unnamed x5, local copies, waits for them, and re-layouts  4.55 us
    dot_general x1, matrix products, one_block(): jnp.einsum('fks,fmk->fms', jac_all, weighted, preferred_element_type=jnp....  3.6 us
  transfers between devices with their start and end apart: 11, of which 7 were waited for; matrix products, arithmetic and copies ran while one was open for 10% of the time, Pallas kernels for 0%

profile of v1, /device:TPU:8, one launch (start us, length us, event | category | flops | bytes accessed | tf_op | source)
XLA Modules:
  0.0 173.4 jit_solution(12073533205643594312)
XLA Ops:
  6.5 1.0 convert_reduce_fusion
  7.5 0.7 multiply_add_fusion
  8.2 0.7 select_reduce_fusion
  9.0 2.2 %collective-permute-start = (s32[3]{0:T(128)S(1)}, s32[3]{0:T(128)S(1)}, u32[]{:S(2)}, u32[]{:S(2)}) collective-permute-start(s32[3]{0:T(128)S(1)} %get-tuple-element.178), channel_id=1, source_target_pairs={{0,254},{2,0},{4,2},{6,4},{8,6},{10,8},{12,10},{14,12},{16,14},{18... | collective-permute-start | bytes 44 | tf_op jit(solution)/shard_map/ppermute | solution.py:13
  11.2 4.3 %collective-permute-start.2 = (s32[3]{0:T(128)S(1)}, s32[3]{0:T(128)S(1)}, u32[]{:S(2)}, u32[]{:S(2)}) collective-permute-start(s32[3]{0:T(128)S(1)} %get-tuple-element.176), channel_id=1, source_target_pairs={{0,4},{2,6},{4,8},{6,10},{8,12},{10,14},{12,16},{14,18},{16,20},{1... | collective-permute-start | bytes 44 | tf_op jit(solution)/shard_map/ppermute | solution.py:13
  15.4 0.1 compare_and_fusion.2
  15.5 0.7 and_bitcast_fusion
  16.2 4.5 %copy.26 = bf16[8,308,411]{1,2,0:T(8,128)(2,1)} copy(bf16[8,308,411]{2,0,1:T(8,128)(2,1)} %param.11) | data formatting | bytes 4050816 | tf_op args[0]
  20.7 2.5 %gather_fusion.2 = bf16[3,128,411]{1,0,2:T(4,128)(2,1)S(1)} fusion(bf16[16,128,411]{1,0,2:T(8,128)(2,1)S(1)} %copy-done, s32[1024]{0:T(1024)S(1)} %pad_clamp_fusion.3), kind=kCustom, calls=%fused_computation.1.clone | custom fusion | bytes 631308 | tf_op jit(solution)/shard_map/jit(_take)/gather | solution.py:35
  23.2 2.5 %gather_fusion.1 = bf16[3,128,411]{1,0,2:T(4,128)(2,1)S(1)} fusion(bf16[16,128,411]{1,0,2:T(8,128)(2,1)S(1)} %copy-done, s32[1024]{0:T(1024)S(1)} %pad_clamp_fusion.4), kind=kCustom, calls=%fused_computation.clone | custom fusion | bytes 631308 | tf_op jit(solution)/shard_map/jit(_take)/gather | solution.py:38
  25.7 1.0 broadcast_select_fusion.3
  26.8 2.5 %gather_fusion.3 = bf16[3,128,411]{1,0,2:T(4,128)(2,1)S(1)} fusion(bf16[16,128,411]{1,0,2:T(8,128)(2,1)S(1)} %copy-done, s32[1024]{0:T(1024)S(1)} %pad_clamp_fusion.2), kind=kCustom, calls=%fused_computation.2.clone | custom fusion | bytes 631308 | tf_op jit(solution)/shard_map/jit(_take)/gather | solution.py:38
  29.3 1.0 broadcast_select_fusion.1
  30.2 4.5 %collective-permute-start.4 = (bf16[3,128,411]{1,0,2:T(4,128)(2,1)}, bf16[3,128,411]{1,0,2:T(4,128)(2,1)S(1)}, u32[]{:S(2)}, u32[]{:S(2)}) collective-permute-start(bf16[3,128,411]{1,0,2:T(4,128)(2,1)} %broadcast_select_fusion.1), channel_id=1, source_target_pairs={{0,254},{2,0},{4,2},{6,4},{8,6},{10,8},{12,10},{14,12},{16,14},{18... | collective-permute-start | bytes 946952 | tf_op jit(solution)/shard_map/ppermute | solution.py:13
  34.8 2.5 %gather_fusion.4 = bf16[3,128,411]{1,0,2:T(4,128)(2,1)S(1)} fusion(bf16[16,128,411]{1,0,2:T(8,128)(2,1)S(1)} %copy-done, s32[1024]{0:T(1024)S(1)} %pad_clamp_fusion.1), kind=kCustom, calls=%fused_computation.3.clone | custom fusion | bytes 631308 | tf_op jit(solution)/shard_map/jit(_take)/gather | solution.py:38
  37.3 0.2 broadcast_select_fusion
  37.5 8.4 %collective-permute-start.5 = (bf16[3,128,411]{1,0,2:T(4,128)(2,1)S(1)}, bf16[3,128,411]{1,0,2:T(4,128)(2,1)S(1)}, u32[]{:S(2)}, u32[]{:S(2)}) collective-permute-start(bf16[3,128,411]{1,0,2:T(4,128)(2,1)S(1)} %broadcast_select_fusion), channel_id=1, source_target_pairs={{0,252},{2,254},{4,0},{6,2},{8,4},{10,6},{12,8},{14,10},{16,12},{1... | collective-permute-start | bytes 946952 | tf_op jit(solution)/shard_map/ppermute | solution.py:13
  45.9 0.2 broadcast_select_fusion.2
  46.1 6.7 %collective-permute-done.4 = bf16[3,128,411]{1,0,2:T(4,128)(2,1)S(1)} collective-permute-done((bf16[3,128,411]{1,0,2:T(4,128)(2,1)}, bf16[3,128,411]{1,0,2:T(4,128)(2,1)S(1)}, u32[]{:S(2)}, u32[]{:S(2)}) %collective-permute-start.4) | collective-permute-done | bytes 315680 | tf_op jit(solution)/shard_map/ppermute | solution.py:13
  52.8 4.7 %collective-permute-done.5 = bf16[3,128,411]{1,0,2:T(4,128)(2,1)S(1)} collective-permute-done((bf16[3,128,411]{1,0,2:T(4,128)(2,1)S(1)}, bf16[3,128,411]{1,0,2:T(4,128)(2,1)S(1)}, u32[]{:S(2)}, u32[]{:S(2)}) %collective-permute-start.5) | collective-permute-done | bytes 315680 | tf_op jit(solution)/shard_map/ppermute | solution.py:13
  57.5 1.4 pad_maximum_fusion
  58.8 0.3 copy.22
  59.1 1.6 gather_fusion
  60.7 3.3 %fusion.7 = bf16[8,128,308]{1,2,0:T(8,128)(2,1)S(1)} fusion(bf16[8,308,411]{1,2,0:T(8,128)(2,1)} %copy.26, bf16[8,128,411]{1,2,0:T(8,128)(2,1)} %gather_fusion, pred[8]{0:T(512)(128)(4,1)S(1)} %get-tuple-element.167, f32[8,308]{1,0:T(8,128)S(1)} %convert_element_type.44), kind=kOutput, calls=%fused_computation.19 | convolution fusion | flops 260303872 | bytes 3507784 | tf_op jit(solution)/shard_map/while/body/fks,fms->fmk/dot_general | solution.py:48
  64.0 0.9 copy.24
  65.0 16.2 %all-gather.4.cloned.1.call-done = bf16[8,128,616]{1,0,2:T(8,128)(2,1)} async-done(((bf16[8,128,308]{1,0,2:T(8,128)(2,1)}), bf16[8,128,616]{1,0,2:T(8,128)(2,1)}) %all-gather.4.cloned.1.call-update) | async-done | bytes 1261584 | tf_op jit(solution)/shard_map/while/body/all_gather | solution.py:52
  81.2 3.6 %fusion.8 = f32[8,128,411]{1,2,0:T(8,128)S(1)} fusion(bf16[8,308,411]{1,2,0:T(8,128)(2,1)} %copy.26, bf16[8,128,616]{1,0,2:T(8,128)(2,1)} %all-gather.4.cloned.1.call-done, bf16[308,616]{1,0:T(8,128)(2,1)} %param.12), kind=kOutput, calls=%fused_computation.21 | convolution fusion | flops 648130560 | bytes 5349888 | tf_op jit(solution)/shard_map/while/body/fks,fmk->fms/dot_general | solution.py:57
  84.8 2.2 %copy.27 = f32[8,128,411]{1,0,2:T(8,128)} copy(f32[8,128,411]{1,2,0:T(8,128)S(1)} %fusion.8) | data formatting | bytes 3366912 | tf_op jit(solution)/shard_map/while/body/fks,fmk->fms/dot_general | solution.py:57
  87.7 17.9 %all-gather.6.cloned.1.call-done = f32[16,128,411]{1,0,2:T(8,128)} async-done(((f32[8,128,411]{1,0,2:T(8,128)}), f32[16,128,411]{1,0,2:T(8,128)}) %all-gather.6.cloned.1.call-update) | async-done | bytes 3366928 | tf_op jit(solution)/shard_map/while/body/all_gather | solution.py:60
  105.5 3.3 %bitcast_reduce_fusion = bf16[8,128,411]{1,0,2:T(8,128)(2,1)} fusion(f32[16,128,411]{1,0,2:T(8,128)} %all-gather.6.cloned.1.call-done), kind=kLoop, calls=%fused_computation.9 | loop fusion | flops 420864 | bytes 4208640 | tf_op jit(solution)/shard_map/while/body/reduce_sum | solution.py:60
  108.9 1.6 copy.29
  110.5 1.1 broadcast_in_dim.58
  111.6 2.0 %while.14 = (s32[]{:T(128)}, bf16[8,128,411]{2,1,0:T(8,128)(2,1)}, s32[]{:T(128)}, s32[]{:T(128)}, bf16[8,128,411]{2,1,0:T(8,128)(2,1)S(1)}, /*index=5*/s32[]{:T(128)}, s32[]{:T(128)}) while((s32[]{:T(128)}, bf16[8,128,411]{2,1,0:T(8,128)(2,1)}, s32[]{:T(128)}, s32[]{:T(128)}, bf16[8,128,411]{2,1,0:T(8,128)(2,1)S(1)}, /*index=5*/s32[]{:T(128)}, ...), condition=%wide.region_4.6_spmd, body=%wide.region_3.5_spmd.sunk | while | flops 420883 | bytes 1683569 | solution.py:65
  111.6 0.7 add_compare_fusion.2
  112.2 1.3 select_convert_fusion.2
  113.6 2.6 %reshape.37 = bf16[8,52608]{1,0:T(8,128)(2,1)S(1)} reshape(bf16[8,128,411]{2,1,0:T(8,128)(2,1)} %get-tuple-element.146) | data formatting | bytes 1683456 | tf_op jit(solution)/shard_map/reshape | solution.py:66
  116.2 0.7 convolution_convert_fusion.1
  116.9 0.7 fusion.21
  117.6 0.9 collective-permute-start.6
  118.4 1.2 collective-permute-start.7
  119.7 4.2 %collective-permute-start.8 = (bf16[3,52608]{1,0:T(4,128)(2,1)S(1)}, bf16[3,52608]{1,0:T(4,128)(2,1)S(1)}, u32[]{:S(2)}, u32[]{:S(2)}) collective-permute-start(bf16[3,52608]{1,0:T(4,128)(2,1)S(1)} %get-tuple-element.172), channel_id=1, source_target_pairs={{0,4},{2,6},{4,8},{6,10},{8,12},{10,14},{12,16},{14,18},{16,20},{1... | collective-permute-start | bytes 946952 | tf_op jit(solution)/shard_map/ppermute | solution.py:13
  123.9 0.1 pad_add_fusion
  124.0 5.5 %collective-permute-done.6 = bf16[3,52608]{1,0:T(4,128)(2,1)S(1)} collective-permute-done((bf16[3,52608]{1,0:T(4,128)(2,1)S(1)}, bf16[3,52608]{1,0:T(4,128)(2,1)S(1)}, u32[]{:S(2)}, u32[]{:S(2)}) %collective-permute-start.6) | collective-permute-done | bytes 315680 | tf_op jit(solution)/shard_map/ppermute | solution.py:13
  129.5 6.8 %collective-permute-done.7 = bf16[3,52608]{1,0:T(4,128)(2,1)S(1)} collective-permute-done((bf16[3,52608]{1,0:T(4,128)(2,1)S(1)}, bf16[3,52608]{1,0:T(4,128)(2,1)S(1)}, u32[]{:S(2)}, u32[]{:S(2)}) %collective-permute-start.7) | collective-permute-done | bytes 315680 | tf_op jit(solution)/shard_map/ppermute | solution.py:13
  136.4 19.4 %collective-permute-done.8 = bf16[3,52608]{1,0:T(4,128)(2,1)S(1)} collective-permute-done((bf16[3,52608]{1,0:T(4,128)(2,1)S(1)}, bf16[3,52608]{1,0:T(4,128)(2,1)S(1)}, u32[]{:S(2)}, u32[]{:S(2)}) %collective-permute-start.8) | collective-permute-done | bytes 315680 | tf_op jit(solution)/shard_map/ppermute | solution.py:13
  155.8 1.4 convolution_convert_fusion
  157.2 5.0 %reshape.38 = bf16[16,128,411]{2,1,0:T(8,128)(2,1)} reshape(bf16[16,52608]{1,0:T(8,128)(2,1)S(1)} %convolution_convert_fusion) | data formatting | bytes 3366912 | tf_op jit(solution)/shard_map/reshape | solution.py:88
  162.2 4.3 %copy.30 = bf16[16,128,411]{1,0,2:T(8,128)(2,1)} copy(bf16[16,128,411]{2,1,0:T(8,128)(2,1)} %reshape.38) | data formatting | bytes 3366912 | tf_op jit(solution)/shard_map/reshape | solution.py:88
  (27 shorter events, 0.2 us)
Async XLA Ops:
  6.5 14.2 %copy-start = (bf16[16,128,411]{1,0,2:T(8,128)(2,1)S(1)}, bf16[16,128,411]{1,0,2:T(8,128)(2,1)}, u32[]{:S(2)}) copy-start(bf16[16,128,411]{1,0,2:T(8,128)(2,1)} %param.14) | copy-start | bytes 5050372
  6.5 74.7 %all-gather.4.cloned.1.call-start = ((), (), s32[]{:S(2)}) async-start(), calls=%async_computation | async-start | bytes 1892352 | tf_op jit(solution)/shard_map/while/body/all_gather | solution.py:52
  9.0 14.2 %collective-permute-start = (s32[3]{0:T(128)S(1)}, s32[3]{0:T(128)S(1)}, u32[]{:S(2)}, u32[]{:S(2)}) collective-permute-start(s32[3]{0:T(128)S(1)} %get-tuple-element.178), channel_id=1, source_target_pairs={{0,254},{2,0},{4,2},{6,4},{8,6},{10,8},{12,10},{14,12},{16,14},{18... | collective-permute-start | bytes 44 | tf_op jit(solution)/shard_map/ppermute | solution.py:13
  11.2 15.6 %collective-permute-start.1 = (s32[3]{0:T(128)S(1)}, s32[3]{0:T(128)S(1)}, u32[]{:S(2)}, u32[]{:S(2)}) collective-permute-start(s32[3]{0:T(128)S(1)} %get-tuple-element.177), channel_id=1, source_target_pairs={{0,2},{2,4},{4,6},{6,8},{8,10},{10,12},{12,14},{14,16},{16,18},{18... | collective-permute-start | bytes 44 | tf_op jit(solution)/shard_map/ppermute | solution.py:13
  11.2 23.6 %collective-permute-start.2 = (s32[3]{0:T(128)S(1)}, s32[3]{0:T(128)S(1)}, u32[]{:S(2)}, u32[]{:S(2)}) collective-permute-start(s32[3]{0:T(128)S(1)} %get-tuple-element.176), channel_id=1, source_target_pairs={{0,4},{2,6},{4,8},{6,10},{8,12},{10,14},{12,16},{14,18},{16,20},{1... | collective-permute-start | bytes 44 | tf_op jit(solution)/shard_map/ppermute | solution.py:13
  16.2 4.6 %copy-start.1 = (bf16[8,308]{1,0:T(8,128)(2,1)S(1)}, bf16[8,308]{1,0:T(8,128)(2,1)}, u32[]{:S(2)}) copy-start(bf16[8,308]{1,0:T(8,128)(2,1)} %param.13) | copy-start | bytes 14788
  26.7 19.4 %collective-permute-start.3 = (bf16[3,128,411]{1,0,2:T(4,128)(2,1)}, bf16[3,128,411]{1,0,2:T(4,128)(2,1)S(1)}, u32[]{:S(2)}, u32[]{:S(2)}) collective-permute-start(bf16[3,128,411]{1,0,2:T(4,128)(2,1)} %broadcast_select_fusion.3), channel_id=1, source_target_pairs={{0,2},{2,4},{4,6},{6,8},{8,10},{10,12},{12,14},{14,16},{16,18},{18... | collective-permute-start | bytes 946952 | tf_op jit(solution)/shard_map/ppermute | solution.py:13
  30.2 22.5 %collective-permute-start.4 = (bf16[3,128,411]{1,0,2:T(4,128)(2,1)}, bf16[3,128,411]{1,0,2:T(4,128)(2,1)S(1)}, u32[]{:S(2)}, u32[]{:S(2)}) collective-permute-start(bf16[3,128,411]{1,0,2:T(4,128)(2,1)} %broadcast_select_fusion.1), channel_id=1, source_target_pairs={{0,254},{2,0},{4,2},{6,4},{8,6},{10,8},{12,10},{14,12},{16,14},{18... | collective-permute-start | bytes 946952 | tf_op jit(solution)/shard_map/ppermute | solution.py:13
  37.5 19.9 %collective-permute-start.5 = (bf16[3,128,411]{1,0,2:T(4,128)(2,1)S(1)}, bf16[3,128,411]{1,0,2:T(4,128)(2,1)S(1)}, u32[]{:S(2)}, u32[]{:S(2)}) collective-permute-start(bf16[3,128,411]{1,0,2:T(4,128)(2,1)S(1)} %broadcast_select_fusion), channel_id=1, source_target_pairs={{0,252},{2,254},{4,0},{6,2},{8,4},{10,6},{12,8},{14,10},{16,12},{1... | collective-permute-start | bytes 946952 | tf_op jit(solution)/shard_map/ppermute | solution.py:13
  64.9 40.6 %all-gather.6.cloned.1.call-start = ((), (), s32[]{:S(2)}) async-start(), calls=%async_computation.1 | async-start | bytes 5050368 | tf_op jit(solution)/shard_map/while/body/all_gather | solution.py:60
  117.6 12.0 %collective-permute-start.6 = (bf16[3,52608]{1,0:T(4,128)(2,1)S(1)}, bf16[3,52608]{1,0:T(4,128)(2,1)S(1)}, u32[]{:S(2)}, u32[]{:S(2)}) collective-permute-start(bf16[3,52608]{1,0:T(4,128)(2,1)S(1)} %get-tuple-element.171), channel_id=1, source_target_pairs={{0,254},{2,0},{4,2},{6,4},{8,6},{10,8},{12,10},{14,12},{16,14},{18... | collective-permute-start | bytes 946952 | tf_op jit(solution)/shard_map/ppermute | solution.py:13
  118.4 17.9 %collective-permute-start.7 = (bf16[3,52608]{1,0:T(4,128)(2,1)S(1)}, bf16[3,52608]{1,0:T(4,128)(2,1)S(1)}, u32[]{:S(2)}, u32[]{:S(2)}) collective-permute-start(bf16[3,52608]{1,0:T(4,128)(2,1)S(1)} %get-tuple-element.173), channel_id=1, source_target_pairs={{0,2},{2,4},{4,6},{6,8},{8,10},{10,12},{12,14},{14,16},{16,18},{18... | collective-permute-start | bytes 946952 | tf_op jit(solution)/shard_map/ppermute | solution.py:13
  119.7 36.1 %collective-permute-start.8 = (bf16[3,52608]{1,0:T(4,128)(2,1)S(1)}, bf16[3,52608]{1,0:T(4,128)(2,1)S(1)}, u32[]{:S(2)}, u32[]{:S(2)}) collective-permute-start(bf16[3,52608]{1,0:T(4,128)(2,1)S(1)} %get-tuple-element.172), channel_id=1, source_target_pairs={{0,4},{2,6},{4,8},{6,10},{8,12},{10,14},{12,16},{14,18},{16,20},{1... | collective-permute-start | bytes 946952 | tf_op jit(solution)/shard_map/ppermute | solution.py:13
Sparse Core Ops, SparseCore 0:
  65.1 16.1 all-gather.3
  87.1 18.3 all-gather.5
